TPU v7x, 512 devices: a whole 4x8x8 slice. The times are simulated.
512 devices in a mesh: band: 32 (over x, y), seq: 16 (over z, core).
Axes of the slice: x: 4, y: 8, z: 8, core: 2. Of those that a mesh axis runs over, the one named last changes fastest.
Arguments:
- posteriors: bfloat16 [32, 262144], P(None, ('band', 'seq'))
- seed_mask: int32 [262144], P(('band', 'seq')), may hold values 0 or 1
- frame_perm: int32 [512, 512], P(('band', 'seq')), may hold values from 0 to 511, each once within a row
- lengths: int32 [256], replicated, may hold values from 1 to 4096, 262144 in all
- embeddings: bfloat16 [262144, 256], P(('band', 'seq')), may hold values from -12 to 12
- partners: int32 [2048, 32], P(('band', 'seq')), may hold values from 0 to 127, as said below
- levels: int32 [2048, 32], P(('band', 'seq')), may hold values from 1 to 8, as said below
Outputs:
- spread_labels: float32 [32, 262144], P(None, ('band', 'seq'))
Inputs may be any that keep to these rules, and one draw needn't show every extreme that they name: `partners`: within each seq index s, slot k pairs the 128 tiles mutually: if tile number a names b in slot k then b names a in slot k; no tile names itself. `levels`: two tiles paired in slot k carry the same level.
All inputs are finite; a program needn't handle non-finite values. No bound on the sum of `seed_mask` on one device may be relied on, other than what follows from the above.
Results may differ from a plain program's by a relative error of at most 0.007.
Values may be sent and summed in bfloat16 or wider, within the bound.
No kernel may reach another device: no remote copies, remote signals or barrier semaphores. Data moves between devices by JAX's collectives and lax.ppermute only.
A program may use at most 64 MiB of HBM per device.

v0:
```python
import math
import jax
import jax.numpy as jnp
from jax import lax
from jax.sharding import PartitionSpec as P

RADIUS = 64
ITERS = 3
decay_len = 16.0
spread_rate = 0.9


def with_halo(cells, sides, width):
    for axis, dim in sides:
        count = lax.axis_size(axis)
        ends = count - 1
        head = lax.slice_in_dim(cells, 0, width, axis=dim)
        tail = lax.slice_in_dim(cells, cells.shape[dim] - width, cells.shape[dim], axis=dim)
        cells = jnp.concatenate(
            [
                lax.ppermute(tail, axis, [(i, (i + 1) % count) for i in range(ends)]),
                cells,
                lax.ppermute(head, axis, [((i + 1) % count, i) for i in range(ends)]),
            ],
            axis=dim,
        )
    return cells


def on_device(posteriors, seed_mask, frame_perm, lengths, embeddings, partners, levels):
    channels, frames = posteriors.shape
    band_count = lax.axis_size("band")
    groups = lax.axis_size("seq")
    tile_count = frames // 128
    seeded = posteriors * seed_mask.astype(jnp.bfloat16)[None, :]
    ordered = jnp.take(seeded, frame_perm[0], axis=1).reshape(
        channels, band_count, frames // band_count
    )
    arrived = lax.all_to_all(ordered, "band", split_axis=1, concat_axis=1, tiled=True)
    labels = arrived.reshape(channels, frames).astype(jnp.float32)
    device = lax.axis_index("band") * groups + lax.axis_index("seq")
    frame_total = frames * band_count * groups
    window = 128 + 2 * RADIUS
    global_at = device * frames - RADIUS + jnp.arange(frames + 2 * RADIUS, dtype=jnp.int32)
    utt_ends = jnp.cumsum(lengths)
    owner_seg = jnp.sum((utt_ends[None, :] <= global_at[:, None]).astype(jnp.int32), axis=1)
    inside = (global_at >= 0) & (global_at < frame_total)
    tile_off = (jnp.arange(tile_count, dtype=jnp.int32) * 128)[:, None, None]
    win_pos = tile_off + jnp.arange(window, dtype=jnp.int32)[None, :, None]
    row_pos = tile_off + RADIUS + jnp.arange(128, dtype=jnp.int32)[None, None, :]
    offset = jnp.abs(win_pos - row_pos)
    linked = (
        (offset >= 1)
        & (offset <= RADIUS)
        & (owner_seg[win_pos] == owner_seg[row_pos])
        & inside[win_pos]
    )
    band_tiles = jnp.where(
        linked, jnp.exp(-offset.astype(jnp.float32) / decay_len), jnp.float32(0.0)
    ).astype(jnp.bfloat16)
    near_degree = jnp.sum(band_tiles.astype(jnp.float32), axis=1).reshape(frames)
    gathered = lax.all_gather(embeddings, "band", axis=0, tiled=True)
    embed_width = embeddings.shape[1]
    partner_rows = gathered.reshape(-1, 128, embed_width)[partners]
    own_rows = embeddings.reshape(tile_count, 128, embed_width)
    inner_prod = jnp.einsum(
        "tkje,tie->tkji", partner_rows, own_rows, preferred_element_type=jnp.float32
    )
    affinity = (
        jnp.exp(0.5 * (inner_prod / math.sqrt(embed_width)))
        * (levels.astype(jnp.float32) / 8.0)[:, :, None, None]
        / 128.0
    )
    affinity = affinity.astype(jnp.bfloat16)
    far_degree = jnp.sum(affinity.astype(jnp.float32), axis=(1, 2)).reshape(frames)
    norm_scale = 1.0 / jnp.sqrt(near_degree + far_degree)

    def squares(residual):
        return lax.psum(jnp.sum(residual * residual, axis=1), ("band", "seq"))

    solution = jnp.zeros((channels, frames), jnp.float32)
    residual = labels
    direction = labels
    norm_now = squares(residual)
    for iteration in range(ITERS):
        lifted = (norm_scale[None, :] * direction).astype(jnp.bfloat16)
        padded = with_halo(lifted, ((("band", "seq"), 1),), RADIUS)
        windows = jnp.stack(
            [padded[:, position * 128 : position * 128 + window] for position in range(tile_count)],
            axis=0,
        )
        near_term = jnp.einsum(
            "tcw,twa->cta", windows, band_tiles, preferred_element_type=jnp.float32
        ).reshape(channels, frames)
        spread = lax.all_gather(lifted, "band", axis=1, tiled=True).reshape(channels, -1, 128)
        far_tiles = spread[:, partners]
        far_term = jnp.einsum(
            "ctkj,tkji->cti", far_tiles, affinity, preferred_element_type=jnp.float32
        ).reshape(channels, frames)
        image = direction - spread_rate * norm_scale[None, :] * (near_term + far_term)
        curve = lax.psum(jnp.sum(direction * image, axis=1), ("band", "seq"))
        alpha = norm_now / curve
        solution = solution + alpha[:, None] * direction
        residual = residual - alpha[:, None] * image
        norm_next = squares(residual)
        direction = residual + (norm_next / norm_now)[:, None] * direction
        norm_now = norm_next
    return solution


def solution(mesh):
    placed = (
        P(None, ("band", "seq")),
        P(("band", "seq")),
        P(("band", "seq"), None),
        P(),
        P(("band", "seq"), None),
        P(("band", "seq"), None),
        P(("band", "seq"), None),
    )
    return jax.shard_map(
        on_device, mesh=mesh, in_specs=placed, out_specs=P(None, ("band", "seq")), check_vma=False
    )
```

profile of v0, /device:TPU:1, one launch (start us, length us, event | category | flops | bytes accessed | tf_op | source)
XLA Modules:
  0.0 862.8 jit_solution(14141777168958132764)
XLA Ops:
  9.4 1.3 reduce.11
  11.5 1.3 gather_fusion
  13.7 10.5 %all-to-all-start = ((bf16[32,2,256]{2,1,0:T(2,128)(2,1)}), bf16[32,2,256]{2,1,0:T(2,128)(2,1)S(1)}, u32[]{:S(2)}, u32[]{:S(2)}) async-start(bf16[32,2,256]{2,1,0:T(2,128)(2,1)} %reshape.489), calls=%async_computation | async-start | bytes 65536 | tf_op jit(solution)/shard_map/all_to_all | solution.py:39
  26.0 4.5 gather_fusion.1
  30.6 2.3 gather_fusion.2
  32.9 6.8 gather_fusion.3
  40.8 78.1 %all-gather.5.cloned.1.call-done = bf16[16384,256]{1,0:T(8,128)(2,1)} async-done(((bf16[512,256]{1,0:T(8,128)(2,1)}), bf16[16384,256]{1,0:T(8,128)(2,1)}) %all-gather.5.cloned.1.call-update) | async-done | bytes 8388624 | tf_op jit(solution)/shard_map/all_gather | solution.py:62
  118.9 10.0 %gather_fusion.4 = bf16[128,128,256]{2,1,0:T(8,128)(2,1)} fusion(bf16[128,128,256]{2,1,0:T(8,128)(2,1)} %bitcast.161, s32[1024]{0:T(1024)S(1)} %pad_clamp_fusion), kind=kCustom, calls=%fused_computation.4 | custom fusion | bytes 16777728 | tf_op jit(solution)/shard_map/gather | solution.py:64
  128.9 7.7 convert_reduce_fusion
  138.1 4.2 collective-permute-start
  142.4 1.9 collective-permute-start.1
  144.4 2.9 collective-permute-done.1
  148.9 58.6 %all-gather.7.cloned.1.call-done = bf16[32,16384]{1,0:T(8,128)(2,1)} async-done(((bf16[32,512]{1,0:T(8,128)(2,1)}), bf16[32,16384]{1,0:T(8,128)(2,1)}) %all-gather.7.cloned.1.call-update) | async-done | bytes 1048592 | tf_op jit(solution)/shard_map/all_gather | solution.py:95
  207.5 1.4 copy_bitcast_fusion.2
  209.7 2.9 fusion.3
  212.9 102.0 %all-reduce = (f32[32]{0:T(128)S(1)}, f32[32]{0:T(128)S(1)}) all-reduce(f32[32]{0:T(128)S(1)} %get-tuple-element.6, f32[32]{0:T(128)S(1)} %get-tuple-element.5), channel_id=1, replica_groups=mesh['band'=32,'seq'=16] {'band','seq'}, use_global_device_ids=true, to_apply=%region_1.2 | all-reduce | flops 64 | bytes 512 | tf_op jit(solution)/shard_map/psum | solution.py:79
  315.1 94.4 %psum.44 = f32[32]{0:T(128)S(1)} all-reduce(f32[32]{0:T(128)S(1)} %multiply_reduce_fusion.2), channel_id=1, replica_groups=mesh['band'=32,'seq'=16] {'band','seq'}, use_global_device_ids=true, to_apply=%region_10.11 | all-reduce | flops 32 | bytes 256 | tf_op jit(solution)/shard_map/psum | solution.py:79
  411.1 3.1 collective-permute-start.2
  414.2 2.1 collective-permute-start.3
  416.3 2.9 collective-permute-done.3
  420.7 57.0 %all-gather.9.cloned.1.call-done = bf16[32,16384]{1,0:T(8,128)(2,1)} async-done(((bf16[32,512]{1,0:T(8,128)(2,1)}), bf16[32,16384]{1,0:T(8,128)(2,1)}) %all-gather.9.cloned.1.call-update) | async-done | bytes 1048592 | tf_op jit(solution)/shard_map/all_gather | solution.py:95
  477.7 1.4 copy_bitcast_fusion.1
  479.9 2.9 fusion.2
  483.1 102.0 %psum.45 = f32[32]{0:T(128)S(1)} all-reduce(f32[32]{0:T(128)S(1)} %multiply_reduce_fusion.1), channel_id=1, replica_groups=mesh['band'=32,'seq'=16] {'band','seq'}, use_global_device_ids=true, to_apply=%region_12.13 | all-reduce | flops 32 | bytes 256 | tf_op jit(solution)/shard_map/psum | solution.py:101
  585.4 94.4 %psum.46 = f32[32]{0:T(128)S(1)} all-reduce(f32[32]{0:T(128)S(1)} %multiply_reduce_fusion), channel_id=1, replica_groups=mesh['band'=32,'seq'=16] {'band','seq'}, use_global_device_ids=true, to_apply=%region_14.15 | all-reduce | flops 32 | bytes 256 | tf_op jit(solution)/shard_map/psum | solution.py:79
  681.3 3.1 collective-permute-start.4
  684.4 1.9 collective-permute-start.5
  686.3 3.0 collective-permute-done.5
  690.9 57.1 %all-gather.11.cloned.1.call-done = bf16[32,16384]{1,0:T(8,128)(2,1)} async-done(((bf16[32,512]{1,0:T(8,128)(2,1)}), bf16[32,16384]{1,0:T(8,128)(2,1)}) %all-gather.11.cloned.1.call-update) | async-done | bytes 1048592 | tf_op jit(solution)/shard_map/all_gather | solution.py:95
  748.0 1.4 copy_bitcast_fusion
  750.1 2.9 fusion.1
  753.5 102.0 %psum.47 = f32[32]{0:T(128)S(1)} all-reduce(f32[32]{0:T(128)S(1)} %fusion.12), channel_id=1, replica_groups=mesh['band'=32,'seq'=16] {'band','seq'}, use_global_device_ids=true, to_apply=%region_16.17 | all-reduce | flops 32 | bytes 256 | tf_op jit(solution)/shard_map/psum | solution.py:101
  (86 shorter events, 20.9 us)
Async XLA Ops:
  6.5 33.2 %copy-start.1 = (s32[4,32]{1,0:T(4,128)S(1)}, s32[4,32]{1,0:T(4,128)}, u32[]{:S(2)}) copy-start(s32[4,32]{1,0:T(4,128)} %param.12) | copy-start | bytes 1540
  6.5 34.0 %copy-start.2 = (s32[4,32]{1,0:T(4,128)S(1)}, s32[4,32]{1,0:T(4,128)}, u32[]{:S(2)}) copy-start(s32[4,32]{1,0:T(4,128)} %param.13) | copy-start | bytes 1540
  6.5 112.4 %all-gather.5.cloned.1.call-start = ((), (), s32[]{:S(2)}) async-start(), calls=%async_computation.1 | async-start | bytes 8650752 | tf_op jit(solution)/shard_map/all_gather | solution.py:62
  13.7 26.9 %all-to-all-start = ((bf16[32,2,256]{2,1,0:T(2,128)(2,1)}), bf16[32,2,256]{2,1,0:T(2,128)(2,1)S(1)}, u32[]{:S(2)}, u32[]{:S(2)}) async-start(bf16[32,2,256]{2,1,0:T(2,128)(2,1)} %reshape.489), calls=%async_computation | async-start | bytes 65536 | tf_op jit(solution)/shard_map/all_to_all | solution.py:39
  24.3 183.2 %all-gather.7.cloned.1.call-start = ((), (), s32[]{:S(2)}) async-start(), calls=%async_computation.2 | async-start | bytes 1081344 | tf_op jit(solution)/shard_map/all_gather | solution.py:95
  118.9 10.0 %copy-start = (bf16[512,256]{1,0:T(8,128)(2,1)S(1)}, bf16[512,256]{1,0:T(8,128)(2,1)}, u32[]{:S(2)}) copy-start(bf16[512,256]{1,0:T(8,128)(2,1)} %param.11) | copy-start | bytes 786436
  137.3 340.4 %all-gather.9.cloned.1.call-start = ((), (), s32[]{:S(2)}) async-start(), calls=%async_computation.3 | async-start | bytes 1081344 | tf_op jit(solution)/shard_map/all_gather | solution.py:95
  138.1 6.3 collective-permute-start
  142.4 5.0 collective-permute-start.1
  410.2 337.7 %all-gather.11.cloned.1.call-start = ((), (), s32[]{:S(2)}) async-start(), calls=%async_computation.4 | async-start | bytes 1081344 | tf_op jit(solution)/shard_map/all_gather | solution.py:95
  411.1 5.2 collective-permute-start.2
  414.2 5.0 collective-permute-start.3
  681.3 5.0 collective-permute-start.4
  684.4 5.0 collective-permute-start.5
Sparse Core Ops, SparseCore 0:
  10.5 108.3 all-gather.4
  137.4 70.0 all-gather.6
  410.4 67.2 all-gather.8
  680.6 67.2 all-gather.10
where the time goes:
time: 864 us; the launch traced here: 863 us
  blocking collectives  495 us (57%)
  waiting for transfers between devices  260 us (30%)
  local copies, waits for them, and re-layouts  36.3 us (4%)
  starting transfers between devices  26.9 us (3%)
  matrix products  18.3 us (2%)
  between operations  13.5 us (2%)
  other arithmetic  12.5 us (1%)
    psum x3, blocking collectives, squares(): return lax.psum(jnp.sum(residual * residual, axis=1), ('band', 'seq'))  291 us
    psum x2, blocking collectives, on_device(): curve = lax.psum(jnp.sum(direction * image, axis=1), ('band', 'seq'))  204 us
    all_gather x3, waiting for transfers between devices, on_device(): lax.all_gather(lifted, 'band', axis=1, tiled=True)  173 us
    all_gather x1, waiting for transfers between devices, on_device(): gathered = lax.all_gather(embeddings, 'band', axis=0, tiled=True)  78.1 us
  transfers between devices with their start and end apart: 11, of which 7 were waited for; matrix products, arithmetic and copies ran while one was open for 3% of the time, Pallas kernels for 0%

commit v1 on v0

--- a/solution.py
+++ b/solution.py
@@ -8,6 +8,11 @@
 ITERS = 3
 decay_len = 16.0
 spread_rate = 0.9
+
+
+def swapped_in(shard, axis, d):
+    sent = jnp.stack([shard] * lax.axis_size(axis))
+    return jnp.concatenate(lax.all_to_all(sent, axis, 0, 0), axis=d)
 
 
 def with_halo(cells, sides, width):
@@ -92,7 +97,7 @@
         near_term = jnp.einsum(
             "tcw,twa->cta", windows, band_tiles, preferred_element_type=jnp.float32
         ).reshape(channels, frames)
-        spread = lax.all_gather(lifted, "band", axis=1, tiled=True).reshape(channels, -1, 128)
+        spread = swapped_in(lifted, "band", 1).reshape(channels, -1, 128)
         far_tiles = spread[:, partners]
         far_term = jnp.einsum(
             "ctkj,tkji->cti", far_tiles, affinity, preferred_element_type=jnp.float32

time: 864 us -> 758 us (0.88)
  waiting for transfers between devices: 260 us -> 131 us
  starting transfers between devices: 26.9 us -> 44.4 us
    all_gather x3 -> x0, waiting for transfers between devices: 173 us -> none  [on_device(): lax.all_gather(lifted, 'band', axis=1, tiled=True)]
    all_to_all x0 -> x3, waiting for transfers between devices: none -> 42.5 us  [swapped_in(): return jnp.concatenate(lax.all_to_all(sent, axis, 0, 0), axis=d)]
    all_to_all x0 -> x3, starting transfers between devices: none -> 17.2 us  [swapped_in(): return jnp.concatenate(lax.all_to_all(sent, axis, 0, 0), axis=d)]
  transfers between devices with their start and end apart: 11 -> 11, of which waited for: 7 -> 7; matrix products, arithmetic and copies ran while one was open for 3% -> 4% of each run, Pallas kernels for 0% -> 0%
where the time goes in v1:
time: 758 us; the launch traced here: 756 us
  blocking collectives  491 us (65%)
  waiting for transfers between devices  131 us (17%)
  starting transfers between devices  44.4 us (6%)
  local copies, waits for them, and re-layouts  39.3 us (5%)
  matrix products  21.3 us (3%)
  other arithmetic  15.8 us (2%)
  between operations  13.9 us (2%)
    psum x3, blocking collectives, squares(): return lax.psum(jnp.sum(residual * residual, axis=1), ('band', 'seq'))  290 us
    psum x2, blocking collectives, on_device(): curve = lax.psum(jnp.sum(direction * image, axis=1), ('band', 'seq'))  201 us
    all_gather x1, waiting for transfers between devices, on_device(): gathered = lax.all_gather(embeddings, 'band', axis=0, tiled=True)  78.2 us
    all_to_all x3, waiting for transfers between devices, swapped_in(): return jnp.concatenate(lax.all_to_all(sent, axis, 0, 0), axis=d)  42.5 us
    all_to_all x3, starting transfers between devices, swapped_in(): return jnp.concatenate(lax.all_to_all(sent, axis, 0, 0), axis=d)  17.2 us
  transfers between devices with their start and end apart: 11, of which 7 were waited for; matrix products, arithmetic and copies ran while one was open for 4% of the time, Pallas kernels for 0%

profile of v1, /device:TPU:1, one launch (start us, length us, event | category | flops | bytes accessed | tf_op | source)
XLA Modules:
  0.0 756.3 jit_solution(10296221404760137009)
XLA Ops:
  13.7 10.5 %all-to-all-start = ((bf16[32,2,256]{2,1,0:T(2,128)(2,1)}), bf16[32,2,256]{2,1,0:T(2,128)(2,1)S(1)}, u32[]{:S(2)}, u32[]{:S(2)}) async-start(bf16[32,2,256]{2,1,0:T(2,128)(2,1)} %reshape.600), calls=%async_computation | async-start | bytes 65536 | tf_op jit(solution)/shard_map/all_to_all | solution.py:44
  25.9 4.5 gather_fusion.1
  30.6 2.3 gather_fusion.2
  32.9 6.8 gather_fusion.3
  40.8 78.2 %all-gather.2.cloned.1.call-done = bf16[16384,256]{1,0:T(8,128)(2,1)} async-done(((bf16[512,256]{1,0:T(8,128)(2,1)}), bf16[16384,256]{1,0:T(8,128)(2,1)}) %all-gather.2.cloned.1.call-update) | async-done | bytes 8388624 | tf_op jit(solution)/shard_map/all_gather | solution.py:67
  119.1 10.0 %gather_fusion.4 = bf16[128,128,256]{2,1,0:T(8,128)(2,1)} fusion(bf16[128,128,256]{2,1,0:T(8,128)(2,1)} %bitcast.149, s32[1024]{0:T(1024)S(1)} %pad_clamp_fusion), kind=kCustom, calls=%fused_computation.4 | custom fusion | bytes 16777728 | tf_op jit(solution)/shard_map/gather | solution.py:69
  129.1 7.7 %convert_reduce_fusion = (f32[4,128]{1,0:T(4,128)S(1)}, bf16[4,32,128,128]{3,2,1,0:T(8,128)(2,1)}) fusion(f32[4,32]{1,0:T(4,128)S(1)} %convert_multiply_fusion.3, bf16[4,32,128,256]{3,2,1,0:T(8,128)(2,1)} %bitcast.150, bf16[4,128,256,1]{2,1,3,0:T(8,128)(2,1)S(1)} %bitcast.164), kind=kOutput, calls=%fused_computation.8 | convolution fusion | flops 1086324224 | bytes 12847616 | tf_op jit(solution)/shard_map/tkje,tie->tkji/dot_general | solution.py:71
  138.4 5.5 all-to-all-start.1
  144.0 4.5 collective-permute-start
  148.5 1.9 collective-permute-start.1
  150.6 3.2 collective-permute-done.1
  154.5 14.2 %all-to-all-done.1 = bf16[32,32,512]{2,1,0:T(8,128)(2,1)S(1)} async-done(((bf16[32,32,512]{2,1,0:T(8,128)(2,1)}), bf16[32,32,512]{2,1,0:T(8,128)(2,1)S(1)}, u32[]{:S(2)}, u32[]{:S(2)}) %all-to-all-start.1) | async-done | bytes 1048608 | tf_op jit(solution)/shard_map/all_to_all | solution.py:15
  171.5 2.9 fusion.3
  174.7 100.9 %all-reduce = (f32[32]{0:T(128)S(1)}, f32[32]{0:T(128)S(1)}) all-reduce(f32[32]{0:T(128)S(1)} %get-tuple-element.6, f32[32]{0:T(128)S(1)} %get-tuple-element.5), channel_id=1, replica_groups=mesh['band'=32,'seq'=16] {'band','seq'}, use_global_device_ids=true, to_apply=%region_1.2 | all-reduce | flops 64 | bytes 512 | tf_op jit(solution)/shard_map/psum | solution.py:84
  275.8 94.4 %psum.44 = f32[32]{0:T(128)S(1)} all-reduce(f32[32]{0:T(128)S(1)} %multiply_reduce_fusion.2), channel_id=1, replica_groups=mesh['band'=32,'seq'=16] {'band','seq'}, use_global_device_ids=true, to_apply=%region_10.11 | all-reduce | flops 32 | bytes 256 | tf_op jit(solution)/shard_map/psum | solution.py:84
  372.2 5.3 all-to-all-start.2
  377.6 3.2 collective-permute-start.2
  380.8 1.9 collective-permute-start.3
  382.7 3.0 collective-permute-done.3
  385.9 2.1 fusion.14
  388.0 14.2 %all-to-all-done.2 = bf16[32,32,512]{2,1,0:T(8,128)(2,1)S(1)} async-done(((bf16[32,32,512]{2,1,0:T(8,128)(2,1)}), bf16[32,32,512]{2,1,0:T(8,128)(2,1)S(1)}, u32[]{:S(2)}, u32[]{:S(2)}) %all-to-all-start.2) | async-done | bytes 1048608 | tf_op jit(solution)/shard_map/all_to_all | solution.py:15
  405.0 2.9 fusion.2
  409.0 100.5 %psum.45 = f32[32]{0:T(128)S(1)} all-reduce(f32[32]{0:T(128)S(1)} %multiply_reduce_fusion.1), channel_id=1, replica_groups=mesh['band'=32,'seq'=16] {'band','seq'}, use_global_device_ids=true, to_apply=%region_12.13 | all-reduce | flops 32 | bytes 256 | tf_op jit(solution)/shard_map/psum | solution.py:106
  511.0 94.4 %psum.46 = f32[32]{0:T(128)S(1)} all-reduce(f32[32]{0:T(128)S(1)} %multiply_reduce_fusion), channel_id=1, replica_groups=mesh['band'=32,'seq'=16] {'band','seq'}, use_global_device_ids=true, to_apply=%region_14.15 | all-reduce | flops 32 | bytes 256 | tf_op jit(solution)/shard_map/psum | solution.py:84
  608.7 6.4 all-to-all-start.3
  615.1 3.2 collective-permute-start.4
  618.4 1.9 collective-permute-start.5
  620.3 3.0 collective-permute-done.5
  623.5 2.1 fusion.15
  625.6 14.1 %all-to-all-done.3 = bf16[32,32,512]{2,1,0:T(8,128)(2,1)S(1)} async-done(((bf16[32,32,512]{2,1,0:T(8,128)(2,1)}), bf16[32,32,512]{2,1,0:T(8,128)(2,1)S(1)}, u32[]{:S(2)}, u32[]{:S(2)}) %all-to-all-start.3) | async-done | bytes 1048608 | tf_op jit(solution)/shard_map/all_to_all | solution.py:15
  642.5 2.9 fusion.1
  646.6 100.6 %psum.47 = f32[32]{0:T(128)S(1)} all-reduce(f32[32]{0:T(128)S(1)} %fusion.12), channel_id=1, replica_groups=mesh['band'=32,'seq'=16] {'band','seq'}, use_global_device_ids=true, to_apply=%region_16.17 | all-reduce | flops 32 | bytes 256 | tf_op jit(solution)/shard_map/psum | solution.py:106
  (126 shorter events, 32.8 us)
Async XLA Ops:
  6.5 33.2 %copy-start.14 = (s32[4,32]{1,0:T(4,128)S(1)}, s32[4,32]{1,0:T(4,128)}, u32[]{:S(2)}) copy-start(s32[4,32]{1,0:T(4,128)} %param.12) | copy-start | bytes 1540
  6.5 34.0 %copy-start.15 = (s32[4,32]{1,0:T(4,128)S(1)}, s32[4,32]{1,0:T(4,128)}, u32[]{:S(2)}) copy-start(s32[4,32]{1,0:T(4,128)} %param.13) | copy-start | bytes 1540
  6.5 112.5 %all-gather.2.cloned.1.call-start = ((), (), s32[]{:S(2)}) async-start(), calls=%async_computation.4 | async-start | bytes 8650752 | tf_op jit(solution)/shard_map/all_gather | solution.py:67
  13.7 26.8 %all-to-all-start = ((bf16[32,2,256]{2,1,0:T(2,128)(2,1)}), bf16[32,2,256]{2,1,0:T(2,128)(2,1)S(1)}, u32[]{:S(2)}, u32[]{:S(2)}) async-start(bf16[32,2,256]{2,1,0:T(2,128)(2,1)} %reshape.600), calls=%async_computation | async-start | bytes 65536 | tf_op jit(solution)/shard_map/all_to_all | solution.py:44
  30.5 123.4 %copy-start.11 = (s32[4,256]{1,0:T(4,128)}, s32[4,256]{1,0:T(4,128)S(1)}, u32[]{:S(2)}) copy-start(s32[4,256]{1,0:T(4,128)S(1)} %eq.17) | copy-start | bytes 12292
  32.9 121.0 %copy-start.16 = (s32[512]{0:T(512)}, s32[512]{0:T(512)S(1)}, u32[]{:S(2)}) copy-start(s32[512]{0:T(512)S(1)} %gather_fusion.2) | copy-start | bytes 6148
  39.7 114.2 %copy-start.17 = (pred[4,256]{1,0:T(4,128)(4,1)}, pred[4,256]{1,0:T(4,128)(4,1)S(1)}, u32[]{:S(2)}) copy-start(pred[4,256]{1,0:T(4,128)(4,1)S(1)} %and.33) | copy-start | bytes 3076
  39.9 114.0 %copy-start.13 = (s32[4,128]{1,0:T(4,128)}, s32[4,128]{1,0:T(4,128)S(1)}, u32[]{:S(2)}) copy-start(s32[4,128]{1,0:T(4,128)S(1)} %iota_add_fusion.2) | copy-start | bytes 6148
  40.0 114.0 %copy-start.10 = (s32[4,256]{1,0:T(4,128)}, s32[4,256]{1,0:T(4,128)S(1)}, u32[]{:S(2)}) copy-start(s32[4,256]{1,0:T(4,128)S(1)} %iota_add_fusion.1) | copy-start | bytes 12292
  40.6 130.1 %copy-start.5 = (s32[1024]{0:T(1024)}, s32[1024]{0:T(1024)S(1)}, u32[]{:S(2)}) copy-start(s32[1024]{0:T(1024)S(1)} %pad_clamp_fusion) | copy-start | bytes 12292
  40.8 96.5 %copy-start.3 = (f32[32,512]{1,0:T(8,128)}, f32[32,512]{1,0:T(8,128)S(1)}, u32[]{:S(2)}) copy-start(f32[32,512]{1,0:T(8,128)S(1)} %copy.61) | copy-start | bytes 196612
  119.1 10.0 %copy-start.4 = (bf16[512,256]{1,0:T(8,128)(2,1)S(1)}, bf16[512,256]{1,0:T(8,128)(2,1)}, u32[]{:S(2)}) copy-start(bf16[512,256]{1,0:T(8,128)(2,1)} %param.11) | copy-start | bytes 786436
  137.3 37.1 %copy-start.6 = (f32[512]{0:T(512)}, f32[512]{0:T(512)S(1)}, u32[]{:S(2)}) copy-start(f32[512]{0:T(512)S(1)} %get-tuple-element.12) | copy-start | bytes 6148
  138.4 30.3 %all-to-all-start.1 = ((bf16[32,32,512]{2,1,0:T(8,128)(2,1)}), bf16[32,32,512]{2,1,0:T(8,128)(2,1)S(1)}, u32[]{:S(2)}, u32[]{:S(2)}) async-start(bf16[32,32,512]{2,1,0:T(8,128)(2,1)} %stack.41), calls=%async_computation.1 | async-start | bytes 2097152 | tf_op jit(solution)/shard_map/all_to_all | solution.py:15
  144.0 6.5 collective-permute-start
  148.5 5.3 collective-permute-start.1
  174.4 197.8 %copy-start.2 = (f32[4,128,32]{1,2,0:T(8,128)}, f32[4,128,32]{1,2,0:T(8,128)S(1)}, u32[]{:S(2)}) copy-start(f32[4,128,32]{1,2,0:T(8,128)S(1)} %fusion.3) | copy-start | bytes 196612
  275.6 96.6 %copy-start.7 = (f32[32]{0:T(128)}, f32[32]{0:T(128)S(1)}, u32[]{:S(2)}) copy-start(f32[32]{0:T(128)S(1)} %div.43) | copy-start | bytes 388
  370.2 2.0 copy-start.19
  370.2 2.0 copy-start.8
  372.2 29.9 %all-to-all-start.2 = ((bf16[32,32,512]{2,1,0:T(8,128)(2,1)}), bf16[32,32,512]{2,1,0:T(8,128)(2,1)S(1)}, u32[]{:S(2)}, u32[]{:S(2)}) async-start(bf16[32,32,512]{2,1,0:T(8,128)(2,1)} %stack.47), calls=%async_computation.2 | async-start | bytes 2097152 | tf_op jit(solution)/shard_map/all_to_all | solution.py:15
  377.6 5.1 collective-permute-start.2
  380.8 5.0 collective-permute-start.3
  408.1 200.6 %copy-start = (f32[32,4,128]{0,2,1:T(8,128)}, f32[32,4,128]{0,2,1:T(8,128)S(1)}, u32[]{:S(2)}) copy-start(f32[32,4,128]{0,2,1:T(8,128)S(1)} %copy.72) | copy-start | bytes 196612
  510.1 98.6 %copy-start.9 = (f32[32]{0:T(128)}, f32[32]{0:T(128)S(1)}, u32[]{:S(2)}) copy-start(f32[32]{0:T(128)S(1)} %div.45) | copy-start | bytes 388
  605.4 3.3 copy-start.18
  606.0 2.7 copy-start.12
  608.7 31.0 %all-to-all-start.3 = ((bf16[32,32,512]{2,1,0:T(8,128)(2,1)}), bf16[32,32,512]{2,1,0:T(8,128)(2,1)S(1)}, u32[]{:S(2)}, u32[]{:S(2)}) async-start(bf16[32,32,512]{2,1,0:T(8,128)(2,1)} %stack.53), calls=%async_computation.3 | async-start | bytes 2097152 | tf_op jit(solution)/shard_map/all_to_all | solution.py:15
  615.1 5.2 collective-permute-start.4
  618.4 5.0 collective-permute-start.5
  640.9 4.7 copy-start.1
Sparse Core Ops, SparseCore 0:
  10.5 108.4 all-gather.1
